TPU v7x, 128 devices: a whole 4x4x4 slice. The times are simulated.
128 devices in a mesh: dp: 4 (over z), outer: 16 (over x, y), inner: 2 (over core).
Axes of the slice: x: 4, y: 4, z: 4, core: 2. Of those that a mesh axis runs over, the one named last changes fastest.
Arguments:
- tokens: bfloat16 [4096, 4096], P(('dp', 'outer', 'inner')), may hold values from -6 to 6
- expert_ids: int32 [4096, 8], P(('dp', 'outer', 'inner')), may hold values from 0 to 31, all different within a row; in each aligned block of 32 rows (0 to 31, 32 to 63, ...) at most 12 rows name the same one
- gate_values: float32 [4096, 8], P(('dp', 'outer', 'inner')), may hold values from 0.02 to 0.5
- upstream: bfloat16 [4096, 4096], P(('dp', 'outer', 'inner')), may hold values from -1.5 to 1.5
- w_gate: bfloat16 [32, 4096, 768], P(('outer', 'inner')), may hold values from -0.09375 to 0.09375
- w_up: bfloat16 [32, 4096, 768], P(('outer', 'inner')), may hold values from -0.09375 to 0.09375
- w_down: bfloat16 [32, 768, 4096], P(('outer', 'inner')), may hold values from -0.21875 to 0.21875
Outputs:
- output: bfloat16 [4096, 4096], P(('dp', 'outer', 'inner'))
- grad_tokens: bfloat16 [4096, 4096], P(('dp', 'outer', 'inner'))
- grad_gates: float32 [4096, 8], P(('dp', 'outer', 'inner'))
- grad_w_gate: bfloat16 [32, 4096, 768], P(('outer', 'inner'), 'dp')
- grad_w_up: bfloat16 [32, 4096, 768], P(('outer', 'inner'), 'dp')
- grad_w_down: bfloat16 [32, 768, 4096], P(('outer', 'inner'), None, 'dp')
Inputs may be any that keep to these rules, and one draw needn't show every extreme that they name: `expert_ids`: each token names 8 different experts. Among the 32 tokens of one device (aligned blocks of rows), no expert is named more than 12 times, a bound that some block reaches.
All inputs are finite; a program needn't handle non-finite values.
Results may differ from a plain program's by a relative error of at most 0.013.
Values may be sent and summed in bfloat16 or wider, within the bound.
No kernel may reach another device: no remote copies, remote signals or barrier semaphores. Data moves between devices by JAX's collectives and lax.ppermute only.
A program may use at most 192 MiB of HBM per device.

v0:
```python
import jax
import jax.numpy as jnp
from jax import lax
from jax.sharding import PartitionSpec as P


def contract_last(left, right):
    return lax.dot_general(
        left, right, (((1,), (1,)), ((), ())), preferred_element_type=jnp.float32
    )


def contract_first(left, right):
    return lax.dot_general(
        left, right, (((0,), (0,)), ((), ())), preferred_element_type=jnp.float32
    )


def expert_rows(rows_in, grads_in, gate_mat, up_mat, down_mat):
    gate_pre = jnp.dot(rows_in, gate_mat, preferred_element_type=jnp.float32)
    up_pre = jnp.dot(rows_in, up_mat, preferred_element_type=jnp.float32)
    sigma = jax.nn.sigmoid(gate_pre)
    silu_value = gate_pre * sigma
    hidden = (silu_value * up_pre).astype(jnp.bfloat16)
    expert_out = jnp.dot(hidden, down_mat, preferred_element_type=jnp.float32).astype(jnp.bfloat16)
    grad_hidden = contract_last(grads_in, down_mat)
    slope = sigma * (1.0 + gate_pre * (1.0 - sigma))
    grad_gate_pre = (grad_hidden * up_pre * slope).astype(jnp.bfloat16)
    grad_up_pre = (grad_hidden * silu_value).astype(jnp.bfloat16)
    pair_grad = (
        contract_last(grad_gate_pre, gate_mat) + contract_last(grad_up_pre, up_mat)
    ).astype(jnp.bfloat16)
    return (hidden, expert_out, grad_gate_pre, grad_up_pre, pair_grad)


def local(tokens, expert_ids, gate_values, upstream, w_gate, w_up, w_down):
    local_tokens = tokens.shape[0]
    width = tokens.shape[1]
    top_count = expert_ids.shape[1]
    ff_width = w_gate.shape[2]
    outer_count = lax.axis_size("outer")
    inner_count = lax.axis_size("inner")
    dp_count = lax.axis_size("dp")
    expert_count = outer_count * inner_count
    group = ("outer", "inner")
    me = lax.axis_index("outer") * inner_count + lax.axis_index("inner")
    group_tokens = expert_count * local_tokens
    capacity = min(local_tokens, 3 * local_tokens * top_count // (2 * expert_count))
    slot_total = expert_count * capacity
    ids_all = lax.all_gather(expert_ids, group, axis=0, tiled=True)
    gates_all = lax.all_gather(gate_values, group, axis=0, tiled=True)
    tokens_all = lax.all_gather(tokens, group, axis=0, tiled=True)
    upstream_all = lax.all_gather(upstream, group, axis=0, tiled=True)
    chosen = ids_all == me
    picked = jnp.any(chosen, axis=1)
    token_gate = jnp.sum(jnp.where(chosen, gates_all, 0.0), axis=1)
    position = jnp.cumsum(picked.astype(jnp.int32)) - 1
    token_slot = jnp.where(picked, position, slot_total)
    slot_token = (
        jnp.full((slot_total + 1,), group_tokens, jnp.int32)
        .at[token_slot]
        .set(jnp.arange(group_tokens, dtype=jnp.int32))[:slot_total]
    )
    token_pad = jnp.concatenate([tokens_all, jnp.zeros((1, width), jnp.bfloat16)], axis=0)
    upstream_pad = jnp.concatenate([upstream_all, jnp.zeros((1, width), jnp.bfloat16)], axis=0)
    gate_pad = jnp.concatenate([token_gate, jnp.zeros((1,), jnp.float32)], axis=0)
    rows_in = token_pad[slot_token]
    up_rows = upstream_pad[slot_token]
    grads_in = (gate_pad[slot_token][:, None] * up_rows.astype(jnp.float32)).astype(jnp.bfloat16)
    hidden, expert_out, grad_gate_pre, grad_up_pre, pair_grad = expert_rows(
        rows_in, grads_in, w_gate[0], w_up[0], w_down[0]
    )
    slot_gates_grad = jnp.sum(up_rows.astype(jnp.float32) * expert_out.astype(jnp.float32), axis=1)
    out_pad = jnp.concatenate([expert_out, jnp.zeros((1, width), jnp.bfloat16)], axis=0)
    back_pad = jnp.concatenate([pair_grad, jnp.zeros((1, width), jnp.bfloat16)], axis=0)
    gg_pad = jnp.concatenate([slot_gates_grad, jnp.zeros((1,), jnp.float32)], axis=0)
    out_share = (token_gate[:, None] * out_pad[token_slot].astype(jnp.float32)).astype(jnp.bfloat16)
    back_share = back_pad[token_slot]
    gg_share = jnp.where(chosen, gg_pad[token_slot][:, None], 0.0)
    output = lax.psum_scatter(out_share, group, scatter_dimension=0, tiled=True)
    grad_tokens = lax.psum_scatter(back_share, group, scatter_dimension=0, tiled=True)
    grad_gates = lax.psum_scatter(gg_share, group, scatter_dimension=0, tiled=True)
    piece = width // dp_count

    def spread_columns(block):
        return lax.all_to_all(
            block.reshape(slot_total, dp_count, piece),
            "dp",
            split_axis=1,
            concat_axis=0,
            tiled=True,
        ).reshape(dp_count * slot_total, piece)

    joined_grads = jnp.concatenate([grad_gate_pre, grad_up_pre], axis=1)
    rows_all = spread_columns(rows_in)
    grads_all = spread_columns(grads_in)
    joined_all = lax.all_gather(joined_grads, "dp", axis=0, tiled=True)
    hidden_all = lax.all_gather(hidden, "dp", axis=0, tiled=True)
    grad_joined = contract_first(rows_all, joined_all)
    grad_down = contract_first(hidden_all, grads_all)
    grad_w_gate = grad_joined[:, :ff_width].astype(jnp.bfloat16)[None]
    grad_w_up = grad_joined[:, ff_width:].astype(jnp.bfloat16)[None]
    grad_w_down = grad_down.astype(jnp.bfloat16)[None]
    return (output, grad_tokens, grad_gates, grad_w_gate, grad_w_up, grad_w_down)


def solution(mesh):
    placed = (
        P(("dp", "outer", "inner"), None),
        P(("dp", "outer", "inner"), None),
        P(("dp", "outer", "inner"), None),
        P(("dp", "outer", "inner"), None),
        P(("outer", "inner"), None, None),
        P(("outer", "inner"), None, None),
        P(("outer", "inner"), None, None),
    )
    return jax.shard_map(
        local,
        mesh=mesh,
        in_specs=placed,
        out_specs=(
            P(("dp", "outer", "inner"), None),
            P(("dp", "outer", "inner"), None),
            P(("dp", "outer", "inner"), None),
            P(("outer", "inner"), "dp", None),
            P(("outer", "inner"), "dp", None),
            P(("outer", "inner"), None, "dp"),
        ),
        check_vma=False,
    )
```

profile of v0, /device:TPU:0, one launch (start us, length us, event | category | flops | bytes accessed | tf_op | source)
XLA Modules:
  0.0 559.8 jit_solution(16613166208065047491)
XLA Ops:
  8.7 25.0 %all-gather = s32[32,32,8]{1,2,0:T(8,128)S(1)} all-gather(s32[1,32,8]{1,2,0:T(8,128)} %bitcast.73), channel_id=1, replica_groups=mesh['dp'=4,'outer'=16,'inner'=2] {'outer','inner'}, dimensions={0}, use_global_device_ids=true | all-gather | bytes 33792 | tf_op jit(solution)/shard_map/all_gather | solution.py:50
  34.5 24.0 %all-gather.1 = f32[32,32,8]{1,2,0:T(8,128)S(1)} all-gather(f32[1,32,8]{1,2,0:T(8,128)} %bitcast.74), channel_id=1, replica_groups=mesh['dp'=4,'outer'=16,'inner'=2] {'outer','inner'}, dimensions={0}, use_global_device_ids=true | all-gather | bytes 33792 | tf_op jit(solution)/shard_map/all_gather | solution.py:51
  66.1 7.7 %concatenate.24 = bf16[1025,4096]{1,0:T(8,128)(2,1)} pad(bf16[1024,4096]{1,0:T(8,128)(2,1)} %all-gather.9.cloned.1.call-done, bf16[]{:T(256)} %constant.7.clone.1), padding=0_1x0_0 | pad | bytes 16785410 | tf_op jit(solution)/shard_map/concatenate | solution.py:65
  73.8 12.8 %gather_fusion.3 = bf16[384,4096]{1,0:T(8,128)(2,1)} fusion(bf16[1025,4096]{1,0:T(8,128)(2,1)} %concatenate.24, s32[1024]{0:T(1024)S(1)} %pad_clamp_fusion), kind=kCustom, calls=%fused_computation.3 | custom fusion | bytes 6292992 | tf_op jit(solution)/shard_map/gather | solution.py:68
  86.6 34.0 %all-gather.7.cloned.1.call-done = bf16[1024,4096]{1,0:T(8,128)(2,1)} async-done(((bf16[32,4096]{1,0:T(8,128)(2,1)}), bf16[1024,4096]{1,0:T(8,128)(2,1)}) %all-gather.7.cloned.1.call-update) | async-done | bytes 8388624 | tf_op jit(solution)/shard_map/all_gather | solution.py:52
  120.6 7.7 %concatenate.21 = bf16[1025,4096]{1,0:T(8,128)(2,1)} pad(bf16[1024,4096]{1,0:T(8,128)(2,1)} %all-gather.7.cloned.1.call-done, bf16[]{:T(256)} %constant.7.clone.1), padding=0_1x0_0 | pad | bytes 16785410 | tf_op jit(solution)/shard_map/concatenate | solution.py:64
  128.3 12.5 %gather_fusion = bf16[384,4096]{1,0:T(8,128)(2,1)S(1)} fusion(bf16[1025,4096]{1,0:T(8,128)(2,1)} %concatenate.21, s32[1024]{0:T(1024)S(1)} %pad_clamp_fusion), kind=kCustom, calls=%fused_computation | custom fusion | bytes 6292992 | tf_op jit(solution)/shard_map/gather | solution.py:67
  140.8 6.5 %fusion.7 = f32[384,768]{1,0:T(8,128)S(1)} fusion(bf16[384,4096]{1,0:T(8,128)(2,1)S(1)} %gather_fusion, bf16[1,4096,768]{2,1,0:T(8,128)(2,1)} %param.12), kind=kOutput, calls=%fused_computation.16 | convolution fusion | flops 2415919104 | bytes 10616832 | tf_op jit(solution)/shard_map/dot_general | solution.py:21
  147.4 5.6 %fusion.1 = f32[384,768]{1,0:T(8,128)S(1)} fusion(bf16[1,768,4096]{2,1,0:T(8,128)(2,1)} %param.13, bf16[384,4096]{1,0:T(8,128)(2,1)S(1)} %copy-done.2, f32[384]{0:T(512)S(1)} %gather_fusion.2), kind=kOutput, calls=%fused_computation.10 | convolution fusion | flops 2420637696 | bytes 10618368 | tf_op jit(solution)/shard_map/dot_general | solution.py:8
  153.1 7.0 %multiply_convert_fusion.4 = (bf16[384,768]{1,0:T(8,128)(2,1)}, bf16[384,768]{1,0:T(8,128)(2,1)}, bf16[384,768]{1,0:T(8,128)(2,1)}) fusion(f32[384,768]{1,0:T(8,128)S(1)} %fusion.1, f32[384,768]{1,0:T(8,128)S(1)} %fusion.7, bf16[384,4096]{1,0:T(8,128)(2,1)S(1)} %gather_fusion, bf16[1,4096,768]{2,1,0:T(8,128)(2,1)} %param.11), kind=kOutput, calls=%fused_computation.36 | convolution fusion | flops 2420342784 | bytes 13565952 | tf_op jit(solution)/shard_map/dot_general | solution.py:20
  160.1 8.2 %multiply_reduce_fusion = (f32[384]{0:T(512)S(1)}, bf16[384,4096]{1,0:T(8,128)(2,1)}) fusion(bf16[384,4096]{1,0:T(8,128)(2,1)} %gather_fusion.3, bf16[384,768]{1,0:T(8,128)(2,1)} %get-tuple-element.12, bf16[1,768,4096]{2,1,0:T(8,128)(2,1)} %param.13), kind=kOutput, calls=%fused_computation.22 | convolution fusion | flops 2423782912 | bytes 13174272 | tf_op jit(solution)/shard_map/dot_general | solution.py:25
  168.3 6.9 %gather_fusion.5 = f32[1024]{0:T(1024)S(1)} fusion(f32[385]{0:T(512)S(1)} %pad_maximum_fusion.2, s32[1024]{0:T(1024)S(1)} %broadcast_clamp_fusion), kind=kCustom, calls=%fused_computation.5 | custom fusion | bytes 12288 | tf_op jit(solution)/shard_map/gather | solution.py:79
  183.0 7.3 %add_convert_fusion = bf16[384,4096]{1,0:T(8,128)(2,1)S(1)} fusion(f32[384,4096]{1,0:T(8,128)S(1)} %fusion.5, bf16[384,768]{1,0:T(8,128)(2,1)S(1)} %copy-done.4, bf16[1,4096,768]{2,1,0:T(8,128)(2,1)} %param.11), kind=kOutput, calls=%fused_computation.23 | convolution fusion | flops 2419064832 | bytes 16318464 | tf_op jit(solution)/shard_map/dot_general | solution.py:8
  190.6 7.8 %gather_fusion.4 = bf16[1024,4096]{1,0:T(8,128)(2,1)} fusion(bf16[385,4096]{1,0:T(8,128)(2,1)S(1)} %concatenate.25, s32[1024]{0:T(1024)S(1)} %broadcast_clamp_fusion), kind=kCustom, calls=%fused_computation.4 | custom fusion | bytes 16781312 | tf_op jit(solution)/shard_map/gather | solution.py:78
  200.6 7.8 %gather_fusion.1 = bf16[1024,4096]{1,0:T(8,128)(2,1)} fusion(bf16[385,4096]{1,0:T(8,128)(2,1)S(1)} %concatenate.22, s32[1024]{0:T(1024)S(1)} %broadcast_clamp_fusion), kind=kCustom, calls=%fused_computation.1 | custom fusion | bytes 16781312 | tf_op jit(solution)/shard_map/gather | solution.py:77
  208.4 10.0 %multiply_convert_fusion = bf16[1024,4096]{1,0:T(8,128)(2,1)} fusion(bf16[1024,4096]{1,0:T(8,128)(2,1)} %gather_fusion.1, f32[1024]{0:T(1024)S(1)} %select_reduce_fusion), kind=kLoop, calls=%fused_computation.7 | loop fusion | flops 12582912 | bytes 16781312 | tf_op jit(solution)/shard_map/convert_element_type | solution.py:77
  230.9 36.1 %all-to-all-done.1 = bf16[384,4,1024]{2,0,1:T(8,128)(2,1)} async-done(((bf16[384,4,1024]{2,0,1:T(8,128)(2,1)}), bf16[384,4,1024]{2,0,1:T(8,128)(2,1)}, u32[]{:S(2)}, u32[]{:S(2)}) %all-to-all-start.1) | async-done | bytes 3145760 | tf_op jit(solution)/shard_map/all_to_all | solution.py:86
  272.4 27.9 %all-gather.13.cloned.1.call-done = bf16[1536,768]{1,0:T(8,128)(2,1)} async-done(((bf16[384,768]{1,0:T(8,128)(2,1)}), bf16[1536,768]{1,0:T(8,128)(2,1)}) %all-gather.13.cloned.1.call-update) | async-done | bytes 2359312 | tf_op jit(solution)/shard_map/all_gather | solution.py:98
  300.3 6.4 %fusion.20 = bf16[1,768,1024]{2,1,0:T(8,128)(2,1)} fusion(bf16[1536,768]{1,0:T(8,128)(2,1)} %all-gather.13.cloned.1.call-done, bf16[1536,1024]{1,0:T(8,128)(2,1)} %bitcast.14), kind=kOutput, calls=%fused_computation.33 | convolution fusion | flops 2416705536 | bytes 7077888 | tf_op jit(solution)/shard_map/dot_general | solution.py:14
  306.7 17.0 %all-to-all-done = bf16[384,4,1024]{2,0,1:T(8,128)(2,1)S(1)} async-done(((bf16[384,4,1024]{2,0,1:T(8,128)(2,1)}), bf16[384,4,1024]{2,0,1:T(8,128)(2,1)S(1)}, u32[]{:S(2)}, u32[]{:S(2)}) %all-to-all-start) | async-done | bytes 3145760 | tf_op jit(solution)/shard_map/all_to_all | solution.py:86
  323.7 35.8 %all-gather.11.cloned.1.call-done = bf16[1536,1536]{1,0:T(8,128)(2,1)} async-done(((bf16[384,1536]{1,0:T(8,128)(2,1)}), bf16[1536,1536]{1,0:T(8,128)(2,1)}) %all-gather.11.cloned.1.call-update) | async-done | bytes 4718608 | tf_op jit(solution)/shard_map/all_gather | solution.py:97
  359.5 7.7 %convolution_convert_fusion = bf16[1024,1536]{1,0:T(8,128)(2,1)S(1)} fusion(bf16[1536,1024]{1,0:T(8,128)(2,1)S(1)} %bitcast.69, bf16[1536,1536]{1,0:T(8,128)(2,1)} %all-gather.11.cloned.1.call-done), kind=kOutput, calls=%fused_computation.26 | convolution fusion | flops 4833411072 | bytes 11010048 | tf_op jit(solution)/shard_map/dot_general | solution.py:14
  369.1 86.9 %reduce-scatter.8.cloned.1.call-done = bf16[32,4096]{1,0:T(8,128)(2,1)} async-done(((bf16[1024,4096]{1,0:T(8,128)(2,1)}), bf16[32,4096]{1,0:T(8,128)(2,1)}) %reduce-scatter.8.cloned.1.call-update) | async-done | bytes 262160 | tf_op jit(solution)/shard_map/reduce_scatter | solution.py:81
  456.0 96.7 %reduce-scatter.6.cloned.1.call-done = bf16[32,4096]{1,0:T(8,128)(2,1)} async-done(((bf16[1024,4096]{1,0:T(8,128)(2,1)}), bf16[32,4096]{1,0:T(8,128)(2,1)}) %reduce-scatter.6.cloned.1.call-update) | async-done | bytes 262160 | tf_op jit(solution)/shard_map/reduce_scatter | solution.py:80
  (64 shorter events, 39.7 us)
Async XLA Ops:
  7.2 58.9 %all-gather.9.cloned.1.call-start = ((), (), s32[]{:S(2)}) async-start(), calls=%async_computation.7 | async-start | bytes 8650752 | tf_op jit(solution)/shard_map/all_gather | solution.py:53
  7.9 112.7 %all-gather.7.cloned.1.call-start = ((), (), s32[]{:S(2)}) async-start(), calls=%async_computation.5 | async-start | bytes 8650752 | tf_op jit(solution)/shard_map/all_gather | solution.py:52
  8.6 262.4 %reduce-scatter.10.cloned.1.call-start = ((), (), s32[]{:S(2)}) async-start(), calls=%async_computation.11 | async-start | bytes 540672
  140.8 12.2 %copy-start = (bf16[384,4096]{1,0:T(8,128)(2,1)}, bf16[384,4096]{1,0:T(8,128)(2,1)S(1)}, u32[]{:S(2)}) copy-start(bf16[384,4096]{1,0:T(8,128)(2,1)S(1)} %gather_fusion) | copy-start | bytes 9437188
  140.8 6.6 %copy-start.2 = (bf16[384,4096]{1,0:T(8,128)(2,1)S(1)}, bf16[384,4096]{1,0:T(8,128)(2,1)}, u32[]{:S(2)}) copy-start(bf16[384,4096]{1,0:T(8,128)(2,1)} %gather_fusion.3) | copy-start | bytes 9437188
  168.3 8.6 %copy-start.4 = (bf16[384,768]{1,0:T(8,128)(2,1)S(1)}, bf16[384,768]{1,0:T(8,128)(2,1)}, u32[]{:S(2)}) copy-start(bf16[384,768]{1,0:T(8,128)(2,1)} %get-tuple-element.10) | copy-start | bytes 1769476
  168.3 8.6 %copy-start.5 = (bf16[384,768]{1,0:T(8,128)(2,1)S(1)}, bf16[384,768]{1,0:T(8,128)(2,1)}, u32[]{:S(2)}) copy-start(bf16[384,768]{1,0:T(8,128)(2,1)} %get-tuple-element.11) | copy-start | bytes 1769476
  176.2 124.1 %all-gather.13.cloned.1.call-start = ((), (), s32[]{:S(2)}) async-start(), calls=%async_computation.10 | async-start | bytes 2949120 | tf_op jit(solution)/shard_map/all_gather | solution.py:98
  176.8 182.7 %all-gather.11.cloned.1.call-start = ((), (), s32[]{:S(2)}) async-start(), calls=%async_computation.9 | async-start | bytes 5898240 | tf_op jit(solution)/shard_map/all_gather | solution.py:97
  178.0 278.0 %reduce-scatter.8.cloned.1.call-start = ((), (), s32[]{:S(2)}) async-start(), calls=%async_computation.8 | async-start | bytes 8650752 | tf_op jit(solution)/shard_map/reduce_scatter | solution.py:81
  198.4 354.4 %reduce-scatter.6.cloned.1.call-start = ((), (), s32[]{:S(2)}) async-start(), calls=%async_computation.6 | async-start | bytes 8650752 | tf_op jit(solution)/shard_map/reduce_scatter | solution.py:80
  218.4 1.9 copy-start.3
  223.8 5.0 copy-start.1
  223.8 43.3 %all-to-all-start.1 = ((bf16[384,4,1024]{2,0,1:T(8,128)(2,1)}), bf16[384,4,1024]{2,0,1:T(8,128)(2,1)}, u32[]{:S(2)}, u32[]{:S(2)}) async-start(bf16[384,4,1024]{2,0,1:T(8,128)(2,1)} %fusion), calls=%async_computation.3 | async-start | bytes 6291456 | tf_op jit(solution)/shard_map/all_to_all | solution.py:86
  267.1 56.6 %all-to-all-start = ((bf16[384,4,1024]{2,0,1:T(8,128)(2,1)}), bf16[384,4,1024]{2,0,1:T(8,128)(2,1)S(1)}, u32[]{:S(2)}, u32[]{:S(2)}) async-start(bf16[384,4,1024]{2,0,1:T(8,128)(2,1)} %bitcast.68), calls=%async_computation.2 | async-start | bytes 6291456 | tf_op jit(solution)/shard_map/all_to_all | solution.py:86
Sparse Core Ops, SparseCore 0:
  10.3 55.5 all-gather.8
  68.1 52.4 all-gather.6
  176.4 76.5 reduce-scatter.9
  255.0 45.2 all-gather.12
  302.4 57.0 all-gather.10
  363.7 92.2 reduce-scatter.7
  460.8 91.9 reduce-scatter.5
where the time goes:
time: 564 us; the launch traced here: 560 us
  waiting for transfers between devices  337 us (60%)
  local copies, waits for them, and re-layouts  81.7 us (14%)
  matrix products  53.7 us (10%)
  blocking collectives  49 us (9%)
  other arithmetic  15.1 us (3%)
  between operations  14.6 us (3%)
  starting transfers between devices  9.13 us (2%)
    reduce_scatter x1, waiting for transfers between devices, local(): output = lax.psum_scatter(out_share, group, scatter_dimension=0, tiled=True)  96.7 us
    reduce_scatter x1, waiting for transfers between devices, local(): lax.psum_scatter(back_share, group, scatter_dimension=0, tiled=True)  86.9 us
    all_to_all x2, waiting for transfers between devices, spread_columns(): lax.all_to_all(block.reshape(slot_total, dp_count, piece), 'dp', split_ax...  53.1 us
    all_gather x1, waiting for transfers between devices, local(): joined_all = lax.all_gather(joined_grads, 'dp', axis=0, tiled=True)  35.8 us
    all_gather x1, waiting for transfers between devices, local(): tokens_all = lax.all_gather(tokens, group, axis=0, tiled=True)  34 us
    all_gather x1, waiting for transfers between devices, local(): hidden_all = lax.all_gather(hidden, 'dp', axis=0, tiled=True)  27.9 us
    all_gather x1, blocking collectives, local(): ids_all = lax.all_gather(expert_ids, group, axis=0, tiled=True)  25 us
    all_gather x1, blocking collectives, local(): gates_all = lax.all_gather(gate_values, group, axis=0, tiled=True)  24 us
  transfers between devices with their start and end apart: 9, of which 7 were waited for; matrix products, arithmetic and copies ran while one was open for 17% of the time, Pallas kernels for 0%

commit v1 on v0

--- a/solution.py
+++ b/solution.py
@@ -94,7 +94,26 @@
     joined_grads = jnp.concatenate([grad_gate_pre, grad_up_pre], axis=1)
     rows_all = spread_columns(rows_in)
     grads_all = spread_columns(grads_in)
-    joined_all = lax.all_gather(joined_grads, "dp", axis=0, tiled=True)
+    size, index, rows = (lax.axis_size("dp"), lax.axis_index("dp"), joined_grads.shape[0])
+    right_2 = [(i, (i + 1) % size) for i in range(size)]
+    backward = [(i, (i - 1) % size) for i in range(size)]
+    filled = jnp.zeros(
+        (*joined_grads.shape[:0], size * rows, *joined_grads.shape[0 + 1 :]), joined_grads.dtype
+    )
+    filled = lax.dynamic_update_slice_in_dim(filled, joined_grads, index * rows, axis=0)
+    from_left = from_right = joined_grads
+    halfway = size // 2
+    for lap in range(1, halfway + 1):
+        from_left = lax.ppermute(from_left, "dp", right_2)
+        filled = lax.dynamic_update_slice_in_dim(
+            filled, from_left, (index - lap) % size * rows, axis=0
+        )
+        if lap < size - halfway:
+            from_right = lax.ppermute(from_right, "dp", backward)
+            filled = lax.dynamic_update_slice_in_dim(
+                filled, from_right, (index + lap) % size * rows, axis=0
+            )
+    joined_all = filled
     hidden_all = lax.all_gather(hidden, "dp", axis=0, tiled=True)
     grad_joined = contract_first(rows_all, joined_all)
     grad_down = contract_first(hidden_all, grads_all)

time: 564 us -> 510 us (0.904)
  waiting for transfers between devices: 337 us -> 270 us
  local copies, waits for them, and re-layouts: 81.7 us -> 90.2 us
    ppermute x0 -> x3, waiting for transfers between devices: none -> 92 us  [the longest x2 92 us: local(): from_left = lax.ppermute(from_left, 'dp', right_2)]
    reduce_scatter x1, waiting for transfers between devices: 86.9 us -> 25.8 us  [local(): lax.psum_scatter(back_share, group, scatter_dimension=0, tiled=True)]
    all_gather x1 -> x0, waiting for transfers between devices: 35.8 us -> none  [local(): joined_all = lax.all_gather(joined_grads, 'dp', axis=0, tiled=True)]
    all_to_all x2, waiting for transfers between devices: 53.1 us -> 19.6 us  [spread_columns(): lax.all_to_all(block.reshape(slot_total, dp_count, piece), 'dp', split_ax...]
    all_gather x1, waiting for transfers between devices: 27.9 us -> 0.01 us  [local(): hidden_all = lax.all_gather(hidden, 'dp', axis=0, tiled=True)]
    dynamic_update_slice x0 -> x3, local copies, waits for them, and re-layouts: none -> 7.26 us  [the longest x2 4.84 us: local(): lax.dynamic_update_slice_in_dim(filled, from_left, (index - lap) % size *...]
  transfers between devices with their start and end apart: 9 -> 11, of which waited for: 7 -> 6; matrix products, arithmetic and copies ran while one was open for 17% -> 20% of each run, Pallas kernels for 0% -> 0%
where the time goes in v1:
time: 510 us; the launch traced here: 506 us
  waiting for transfers between devices  270 us (53%)
  local copies, waits for them, and re-layouts  90.2 us (18%)
  matrix products  54 us (11%)
  blocking collectives  49 us (10%)
  other arithmetic  15.3 us (3%)
  between operations  14.7 us (3%)
  starting transfers between devices  12.8 us (3%)
    reduce_scatter x1, waiting for transfers between devices, local(): output = lax.psum_scatter(out_share, group, scatter_dimension=0, tiled=True)  96.6 us
    ppermute x2, waiting for transfers between devices, local(): from_left = lax.ppermute(from_left, 'dp', right_2)  92 us
    all_gather x1, waiting for transfers between devices, local(): tokens_all = lax.all_gather(tokens, group, axis=0, tiled=True)  34 us
    reduce_scatter x1, waiting for transfers between devices, local(): lax.psum_scatter(back_share, group, scatter_dimension=0, tiled=True)  25.8 us
    all_gather x1, blocking collectives, local(): ids_all = lax.all_gather(expert_ids, group, axis=0, tiled=True)  25 us
    all_gather x1, blocking collectives, local(): gates_all = lax.all_gather(gate_values, group, axis=0, tiled=True)  24 us
    all_to_all x2, waiting for transfers between devices, spread_columns(): lax.all_to_all(block.reshape(slot_total, dp_count, piece), 'dp', split_ax...  19.6 us
    dot_general x3, matrix products, contract_last(): lax.dot_general(left, right, (((1,), (1,)), ((), ())), preferred_element_...  17.9 us
  transfers between devices with their start and end apart: 11, of which 6 were waited for; matrix products, arithmetic and copies ran while one was open for 20% of the time, Pallas kernels for 0%

profile of v1, /device:TPU:0, one launch (start us, length us, event | category | flops | bytes accessed | tf_op | source)
XLA Modules:
  0.0 506.0 jit_solution(10604069170392813584)
XLA Ops:
  8.7 25.0 %all-gather = s32[32,32,8]{1,2,0:T(8,128)S(1)} all-gather(s32[1,32,8]{1,2,0:T(8,128)} %bitcast.73), channel_id=1, replica_groups=mesh['dp'=4,'outer'=16,'inner'=2] {'outer','inner'}, dimensions={0}, use_global_device_ids=true | all-gather | bytes 33792 | tf_op jit(solution)/shard_map/all_gather | solution.py:50
  34.5 24.0 %all-gather.1 = f32[32,32,8]{1,2,0:T(8,128)S(1)} all-gather(f32[1,32,8]{1,2,0:T(8,128)} %bitcast.74), channel_id=1, replica_groups=mesh['dp'=4,'outer'=16,'inner'=2] {'outer','inner'}, dimensions={0}, use_global_device_ids=true | all-gather | bytes 33792 | tf_op jit(solution)/shard_map/all_gather | solution.py:51
  66.1 7.7 %concatenate.24 = bf16[1025,4096]{1,0:T(8,128)(2,1)} pad(bf16[1024,4096]{1,0:T(8,128)(2,1)} %all-gather.8.cloned.1.call-done, bf16[]{:T(256)} %constant.55.clone.1), padding=0_1x0_0 | pad | bytes 16785410 | tf_op jit(solution)/shard_map/concatenate | solution.py:65
  73.8 12.8 %gather_fusion.3 = bf16[384,4096]{1,0:T(8,128)(2,1)} fusion(bf16[1025,4096]{1,0:T(8,128)(2,1)} %concatenate.24, s32[1024]{0:T(1024)S(1)} %pad_clamp_fusion), kind=kCustom, calls=%fused_computation.3 | custom fusion | bytes 6292992 | tf_op jit(solution)/shard_map/gather | solution.py:68
  86.6 34.0 %all-gather.6.cloned.1.call-done = bf16[1024,4096]{1,0:T(8,128)(2,1)} async-done(((bf16[32,4096]{1,0:T(8,128)(2,1)}), bf16[1024,4096]{1,0:T(8,128)(2,1)}) %all-gather.6.cloned.1.call-update) | async-done | bytes 8388624 | tf_op jit(solution)/shard_map/all_gather | solution.py:52
  120.6 7.7 %concatenate.21 = bf16[1025,4096]{1,0:T(8,128)(2,1)} pad(bf16[1024,4096]{1,0:T(8,128)(2,1)} %all-gather.6.cloned.1.call-done, bf16[]{:T(256)} %constant.55.clone.1), padding=0_1x0_0 | pad | bytes 16785410 | tf_op jit(solution)/shard_map/concatenate | solution.py:64
  128.3 12.5 %gather_fusion = bf16[384,4096]{1,0:T(8,128)(2,1)S(1)} fusion(bf16[1025,4096]{1,0:T(8,128)(2,1)} %concatenate.21, s32[1024]{0:T(1024)S(1)} %pad_clamp_fusion), kind=kCustom, calls=%fused_computation | custom fusion | bytes 6292992 | tf_op jit(solution)/shard_map/gather | solution.py:67
  140.8 6.5 %fusion.7 = f32[384,768]{1,0:T(8,128)S(1)} fusion(bf16[384,4096]{1,0:T(8,128)(2,1)S(1)} %gather_fusion, bf16[1,4096,768]{2,1,0:T(8,128)(2,1)} %param.12), kind=kOutput, calls=%fused_computation.16 | convolution fusion | flops 2415919104 | bytes 10616832 | tf_op jit(solution)/shard_map/dot_general | solution.py:21
  147.4 5.6 %fusion.1 = f32[384,768]{1,0:T(8,128)S(1)} fusion(bf16[1,768,4096]{2,1,0:T(8,128)(2,1)} %param.13, bf16[384,4096]{1,0:T(8,128)(2,1)S(1)} %copy-done.2, f32[384]{0:T(512)S(1)} %gather_fusion.2), kind=kOutput, calls=%fused_computation.10 | convolution fusion | flops 2420637696 | bytes 10618368 | tf_op jit(solution)/shard_map/dot_general | solution.py:8
  153.1 7.0 %multiply_convert_fusion.4 = (bf16[384,768]{1,0:T(8,128)(2,1)}, bf16[384,768]{1,0:T(8,128)(2,1)}, bf16[384,768]{1,0:T(8,128)(2,1)}) fusion(f32[384,768]{1,0:T(8,128)S(1)} %fusion.1, f32[384,768]{1,0:T(8,128)S(1)} %fusion.7, bf16[384,4096]{1,0:T(8,128)(2,1)S(1)} %gather_fusion, bf16[1,4096,768]{2,1,0:T(8,128)(2,1)} %param.11), kind=kOutput, calls=%fused_computation.36 | convolution fusion | flops 2420342784 | bytes 13565952 | tf_op jit(solution)/shard_map/dot_general | solution.py:20
  160.1 8.2 %multiply_reduce_fusion = (f32[384]{0:T(512)S(1)}, bf16[384,4096]{1,0:T(8,128)(2,1)}) fusion(bf16[384,4096]{1,0:T(8,128)(2,1)} %gather_fusion.3, bf16[384,768]{1,0:T(8,128)(2,1)} %get-tuple-element.12, bf16[1,768,4096]{2,1,0:T(8,128)(2,1)} %param.13), kind=kOutput, calls=%fused_computation.22 | convolution fusion | flops 2423782912 | bytes 13174272 | tf_op jit(solution)/shard_map/dot_general | solution.py:25
  168.3 6.9 %gather_fusion.5 = f32[1024]{0:T(1024)S(1)} fusion(f32[385]{0:T(512)S(1)} %pad_maximum_fusion.2, s32[1024]{0:T(1024)S(1)} %broadcast_clamp_fusion), kind=kCustom, calls=%fused_computation.5 | custom fusion | bytes 12288 | tf_op jit(solution)/shard_map/gather | solution.py:79
  176.9 4.9 fusion.5
  181.8 7.3 %add_convert_fusion = bf16[384,4096]{1,0:T(8,128)(2,1)S(1)} fusion(f32[384,4096]{1,0:T(8,128)S(1)} %fusion.5, bf16[384,768]{1,0:T(8,128)(2,1)S(1)} %copy-done.5, bf16[1,4096,768]{2,1,0:T(8,128)(2,1)} %param.11), kind=kOutput, calls=%fused_computation.23 | convolution fusion | flops 2419064832 | bytes 16318464 | tf_op jit(solution)/shard_map/dot_general | solution.py:8
  189.4 7.8 %gather_fusion.4 = bf16[1024,4096]{1,0:T(8,128)(2,1)} fusion(bf16[385,4096]{1,0:T(8,128)(2,1)S(1)} %concatenate.25, s32[1024]{0:T(1024)S(1)} %broadcast_clamp_fusion), kind=kCustom, calls=%fused_computation.4 | custom fusion | bytes 16781312 | tf_op jit(solution)/shard_map/gather | solution.py:78
  199.4 7.8 %gather_fusion.1 = bf16[1024,4096]{1,0:T(8,128)(2,1)} fusion(bf16[385,4096]{1,0:T(8,128)(2,1)S(1)} %concatenate.22, s32[1024]{0:T(1024)S(1)} %broadcast_clamp_fusion), kind=kCustom, calls=%fused_computation.1 | custom fusion | bytes 16781312 | tf_op jit(solution)/shard_map/gather | solution.py:77
  207.2 10.0 %multiply_convert_fusion = bf16[1024,4096]{1,0:T(8,128)(2,1)} fusion(bf16[1024,4096]{1,0:T(8,128)(2,1)} %gather_fusion.1, f32[1024]{0:T(1024)S(1)} %select_reduce_fusion), kind=kLoop, calls=%fused_computation.7 | loop fusion | flops 12582912 | bytes 16781312 | tf_op jit(solution)/shard_map/convert_element_type | solution.py:77
  231.4 76.4 %collective-permute-done = bf16[384,1536]{1,0:T(8,128)(2,1)} collective-permute-done((bf16[384,1536]{1,0:T(8,128)(2,1)}, bf16[384,1536]{1,0:T(8,128)(2,1)}, u32[]{:S(2)}, u32[]{:S(2)}) %collective-permute-start) | collective-permute-done | bytes 1179680 | tf_op jit(solution)/shard_map/ppermute | solution.py:107
  322.5 15.7 %collective-permute-done.2 = bf16[384,1536]{1,0:T(8,128)(2,1)} collective-permute-done((bf16[384,1536]{1,0:T(8,128)(2,1)}, bf16[384,1536]{1,0:T(8,128)(2,1)}, u32[]{:S(2)}, u32[]{:S(2)}) %collective-permute-start.2) | collective-permute-done | bytes 1179680 | tf_op jit(solution)/shard_map/ppermute | solution.py:107
  340.6 7.9 %convolution_convert_fusion = bf16[1024,1536]{1,0:T(8,128)(2,1)S(1)} fusion(bf16[1536,1024]{1,0:T(8,128)(2,1)S(1)} %bitcast.69, bf16[1536,1536]{1,0:T(8,128)(2,1)} %constant_dynamic-update-slice_fusion), kind=kOutput, calls=%fused_computation.26 | convolution fusion | flops 4833411072 | bytes 11010048 | tf_op jit(solution)/shard_map/dot_general | solution.py:14
  350.4 19.6 %all-to-all-done.1 = bf16[384,4,1024]{2,0,1:T(8,128)(2,1)} async-done(((bf16[384,4,1024]{2,0,1:T(8,128)(2,1)}), bf16[384,4,1024]{2,0,1:T(8,128)(2,1)}, u32[]{:S(2)}, u32[]{:S(2)}) %all-to-all-start.1) | async-done | bytes 3145760 | tf_op jit(solution)/shard_map/all_to_all | solution.py:86
  369.9 6.5 %fusion.20 = bf16[1,768,1024]{2,1,0:T(8,128)(2,1)} fusion(bf16[1536,768]{1,0:T(8,128)(2,1)} %all-gather.10.cloned.1.call-done, bf16[1536,1024]{1,0:T(8,128)(2,1)} %bitcast.14), kind=kOutput, calls=%fused_computation.33 | convolution fusion | flops 2416705536 | bytes 7077888 | tf_op jit(solution)/shard_map/dot_general | solution.py:14
  376.5 25.8 %reduce-scatter.8.cloned.1.call-done = bf16[32,4096]{1,0:T(8,128)(2,1)} async-done(((bf16[1024,4096]{1,0:T(8,128)(2,1)}), bf16[32,4096]{1,0:T(8,128)(2,1)}) %reduce-scatter.8.cloned.1.call-update) | async-done | bytes 262160 | tf_op jit(solution)/shard_map/reduce_scatter | solution.py:81
  402.3 96.6 %reduce-scatter.6.cloned.1.call-done = bf16[32,4096]{1,0:T(8,128)(2,1)} async-done(((bf16[1024,4096]{1,0:T(8,128)(2,1)}), bf16[32,4096]{1,0:T(8,128)(2,1)}) %reduce-scatter.6.cloned.1.call-update) | async-done | bytes 262160 | tf_op jit(solution)/shard_map/reduce_scatter | solution.py:80
  (77 shorter events, 47.0 us)
Async XLA Ops:
  7.2 58.9 %all-gather.8.cloned.1.call-start = ((), (), s32[]{:S(2)}) async-start(), calls=%async_computation.7 | async-start | bytes 8650752 | tf_op jit(solution)/shard_map/all_gather | solution.py:53
  7.9 112.7 %all-gather.6.cloned.1.call-start = ((), (), s32[]{:S(2)}) async-start(), calls=%async_computation.5 | async-start | bytes 8650752 | tf_op jit(solution)/shard_map/all_gather | solution.py:52
  8.6 307.6 %reduce-scatter.10.cloned.1.call-start = ((), (), s32[]{:S(2)}) async-start(), calls=%async_computation.10 | async-start | bytes 540672
  140.8 12.2 %copy-start = (bf16[384,4096]{1,0:T(8,128)(2,1)}, bf16[384,4096]{1,0:T(8,128)(2,1)S(1)}, u32[]{:S(2)}) copy-start(bf16[384,4096]{1,0:T(8,128)(2,1)S(1)} %gather_fusion) | copy-start | bytes 9437188
  140.8 6.6 %copy-start.2 = (bf16[384,4096]{1,0:T(8,128)(2,1)S(1)}, bf16[384,4096]{1,0:T(8,128)(2,1)}, u32[]{:S(2)}) copy-start(bf16[384,4096]{1,0:T(8,128)(2,1)} %gather_fusion.3) | copy-start | bytes 9437188
  168.3 8.6 %copy-start.7 = (bf16[384,768]{1,0:T(8,128)(2,1)S(1)}, bf16[384,768]{1,0:T(8,128)(2,1)}, u32[]{:S(2)}) copy-start(bf16[384,768]{1,0:T(8,128)(2,1)} %get-tuple-element.11) | copy-start | bytes 1769476
  176.2 193.7 %all-gather.10.cloned.1.call-start = ((), (), s32[]{:S(2)}) async-start(), calls=%async_computation.9 | async-start | bytes 2949120 | tf_op jit(solution)/shard_map/all_gather | solution.py:117
  176.8 225.5 %reduce-scatter.8.cloned.1.call-start = ((), (), s32[]{:S(2)}) async-start(), calls=%async_computation.8 | async-start | bytes 8650752 | tf_op jit(solution)/shard_map/reduce_scatter | solution.py:81
  176.9 5.0 copy-start.5
  197.2 301.7 %reduce-scatter.6.cloned.1.call-start = ((), (), s32[]{:S(2)}) async-start(), calls=%async_computation.6 | async-start | bytes 8650752 | tf_op jit(solution)/shard_map/reduce_scatter | solution.py:80
  217.2 1.9 copy-start.1
  221.2 90.0 %all-to-all-start = ((bf16[384,4,1024]{2,0,1:T(8,128)(2,1)}), bf16[384,4,1024]{2,0,1:T(8,128)(2,1)S(1)}, u32[]{:S(2)}, u32[]{:S(2)}) async-start(bf16[384,4,1024]{2,0,1:T(8,128)(2,1)} %bitcast.68), calls=%async_computation.2 | async-start | bytes 6291456 | tf_op jit(solution)/shard_map/all_to_all | solution.py:86
  225.7 1.1 copy-start.6
  225.7 1.2 copy-start.8
  225.7 82.0 %copy-start.3 = (bf16[384,4096]{1,0:T(8,128)(2,1)S(1)}, bf16[384,4096]{1,0:T(8,128)(2,1)}, u32[]{:S(2)}) copy-start(bf16[384,4096]{1,0:T(8,128)(2,1)} %gather_fusion.3) | copy-start | bytes 9437188
  228.1 79.6 %copy-start.4 = (bf16[1536,1536]{1,0:T(8,128)(2,1)}, bf16[1536,1536]{1,0:T(8,128)(2,1)S(1)}, u32[]{:S(2)}) copy-start(bf16[1536,1536]{1,0:T(8,128)(2,1)S(1)} %get-tuple-element.14) | copy-start | bytes 14155780
  228.1 79.6 %collective-permute-start = (bf16[384,1536]{1,0:T(8,128)(2,1)}, bf16[384,1536]{1,0:T(8,128)(2,1)}, u32[]{:S(2)}, u32[]{:S(2)}) collective-permute-start(bf16[384,1536]{1,0:T(8,128)(2,1)} %get-tuple-element.13), channel_id=1, source_target_pairs={{0,32},{32,64},{64,96},{96,0},{1,33},{33,65},{65,97},{97,1},{2,34}... | collective-permute-start | bytes 3538952 | tf_op jit(solution)/shard_map/ppermute | solution.py:107
  230.1 89.9 %collective-permute-start.1 = (bf16[384,1536]{1,0:T(8,128)(2,1)}, bf16[384,1536]{1,0:T(8,128)(2,1)}, u32[]{:S(2)}, u32[]{:S(2)}) collective-permute-start(bf16[384,1536]{1,0:T(8,128)(2,1)} %get-tuple-element.13), channel_id=1, source_target_pairs={{0,96},{32,0},{64,32},{96,64},{1,97},{33,1},{65,33},{97,65},{2,98}... | collective-permute-start | bytes 3538952 | tf_op jit(solution)/shard_map/ppermute | solution.py:112
  307.7 30.4 %collective-permute-start.2 = (bf16[384,1536]{1,0:T(8,128)(2,1)}, bf16[384,1536]{1,0:T(8,128)(2,1)}, u32[]{:S(2)}, u32[]{:S(2)}) collective-permute-start(bf16[384,1536]{1,0:T(8,128)(2,1)} %collective-permute-done), channel_id=1, source_target_pairs={{0,32},{32,64},{64,96},{96,0},{1,33},{33,65},{65,97},{97,1},{2,34}... | collective-permute-start | bytes 3538952 | tf_op jit(solution)/shard_map/ppermute | solution.py:107
  311.3 58.6 %all-to-all-start.1 = ((bf16[384,4,1024]{2,0,1:T(8,128)(2,1)}), bf16[384,4,1024]{2,0,1:T(8,128)(2,1)}, u32[]{:S(2)}, u32[]{:S(2)}) async-start(bf16[384,4,1024]{2,0,1:T(8,128)(2,1)} %fusion), calls=%async_computation.3 | async-start | bytes 6291456 | tf_op jit(solution)/shard_map/all_to_all | solution.py:86
Sparse Core Ops, SparseCore 0:
  10.3 55.5 all-gather.7
  68.1 52.4 all-gather.5
  176.3 76.4 reduce-scatter.9
  254.4 51.7 all-gather.9
  310.3 91.9 reduce-scatter.7
  406.9 91.9 reduce-scatter.5
